TPU v7x, 32 devices: a whole 2x2x4 slice. The times are simulated.
32 devices in a mesh: rep: 4 (over y, x), shard: 8 (over z, core).
Axes of the slice: x: 2, y: 2, z: 4, core: 2. Of those that a mesh axis runs over, the one named last changes fastest.
Arguments:
- activations: bfloat16 [49152, 1280], P(('rep', 'shard')), may hold values from -6 to 6
- cotangents: bfloat16 [49152, 1280], P(('rep', 'shard')), may hold values from -6 to 6
- grad_vectors: bfloat16 [32, 2, 1280], P(('rep', 'shard')), may hold values from -448 to 448
- master_matrix: float32 [1280, 1280], P('shard'), may hold values from -600 to 600
- first_matrix: float32 [1280, 1280], P('shard'), may hold values from -800 to 800
- second_matrix: float32 [1280, 1280], P('shard'), may hold values from 0.3 to 3.2
- master_vector: float32 [2, 1280], P(None, 'shard'), may hold values from 0.05 to 1
- first_vector: float32 [2, 1280], P(None, 'shard'), may hold values from -4 to 4
- second_vector: float32 [2, 1280], P(None, 'shard'), may hold values from 0.1 to 1
Outputs:
- gathered_matrix: bfloat16 [1280, 1280], replicated
- gathered_vectors: bfloat16 [2, 1280], replicated
- master_rows: float32 [1280, 1280], P('shard')
- first_rows: float32 [1280, 1280], P('shard')
- second_rows: float32 [1280, 1280], P('shard')
- master_vectors: float32 [2, 1280], P(None, 'shard')
- first_vectors: float32 [2, 1280], P(None, 'shard')
- second_vectors: float32 [2, 1280], P(None, 'shard')
All inputs are finite; a program needn't handle non-finite values.
Results may differ from a plain program's by a relative error of at most 0.0004.
Values may be sent and summed in bfloat16 or wider, within the bound.
No kernel may reach another device: no remote copies, remote signals or barrier semaphores. Data moves between devices by JAX's collectives and lax.ppermute only.
A program may use at most 64 MiB of HBM per device.

v0:
```python
import math

import jax
import jax.numpy as jnp
from jax import lax
from jax.sharding import PartitionSpec as P

beta_one = 0.9
beta_two = 0.95
adam_eps = 1e-08
decay_rate = 0.1
learn_rate = 0.2
bias_one = 0.9999734386011124
bias_two = 0.994079470779666
norm_eps = 1e-06


def moments(gradient, moment_one, moment_two):
    fresh_one = beta_one * moment_one + (1.0 - beta_one) * gradient
    fresh_two = beta_two * moment_two + (1.0 - beta_two) * gradient * gradient
    return (fresh_one, fresh_two)


def direction_of(fresh_one, fresh_two, master):
    return fresh_one / bias_one / (jnp.sqrt(fresh_two / bias_two) + adam_eps) + decay_rate * master


def per_device(
    activations,
    cotangents,
    grad_vectors,
    master_matrix,
    first_matrix,
    second_matrix,
    master_vector,
    first_vector,
    second_vector,
):
    rep_count = lax.axis_size("rep")
    shard_count = lax.axis_size("shard")
    tok_count, model_width = activations.shape
    grad_scale = 1.0 / math.sqrt(tok_count * rep_count * shard_count)
    weight_sq = jnp.sum(master_matrix * master_matrix)
    vector_sq = jnp.sum(master_vector * master_vector, axis=1)
    weight_tot, vector_tot = lax.psum((weight_sq, vector_sq), "shard")
    vector_term = grad_vectors[0].astype(jnp.float32).T * grad_scale
    contract = (((0,), (0,)), ((), ()))
    grad_term = (
        lax.dot_general(cotangents, activations, contract, preferred_element_type=jnp.float32)
        * grad_scale
    )
    shard_grad, shard_vector = (
        lax.psum_scatter(grad_term, "shard", scatter_dimension=0, tiled=True),
        lax.psum_scatter(vector_term, "shard", scatter_dimension=0, tiled=True),
    )
    grad_rows, grad_columns = lax.psum((shard_grad, shard_vector), "rep")
    grad_vecs = grad_columns.T
    first_rows, second_rows = moments(grad_rows, first_matrix, second_matrix)
    first_vecs, second_vecs = moments(grad_vecs, first_vector, second_vector)
    update_matrix = direction_of(first_rows, second_rows, master_matrix)
    update_vec = direction_of(first_vecs, second_vecs, master_vector)
    update_sq = jnp.sum(update_matrix * update_matrix)
    upvector_sq = jnp.sum(update_vec * update_vec, axis=1)
    update_tot, upvector_tot = lax.psum((update_sq, upvector_sq), "shard")
    trust_matrix = jnp.sqrt(weight_tot) / jnp.sqrt(update_tot + norm_eps)
    trust_vec = (jnp.sqrt(vector_tot) / jnp.sqrt(upvector_tot + norm_eps))[:, None]
    stepped = master_matrix - learn_rate * trust_matrix * update_matrix
    master_rows = stepped / jnp.sqrt(jnp.mean(stepped * stepped, axis=1, keepdims=True) + norm_eps)
    master_vecs = master_vector - learn_rate * trust_vec * update_vec
    gathered_matrix, gathered_vectors = (
        lax.all_gather(master_rows.astype(jnp.bfloat16), "shard", axis=0, tiled=True),
        lax.all_gather(master_vecs.astype(jnp.bfloat16), "shard", axis=1, tiled=True),
    )
    return (
        gathered_matrix,
        gathered_vectors,
        master_rows,
        first_rows,
        second_rows,
        master_vecs,
        first_vecs,
        second_vecs,
    )


def solution(mesh):
    placed = (
        P(("rep", "shard"), None),
        P(("rep", "shard"), None),
        P(("rep", "shard"), None, None),
        P("shard", None),
        P("shard", None),
        P("shard", None),
        P(None, "shard"),
        P(None, "shard"),
        P(None, "shard"),
    )
    return jax.shard_map(
        per_device,
        mesh=mesh,
        in_specs=placed,
        out_specs=(
            P(),
            P(),
            P("shard", None),
            P("shard", None),
            P("shard", None),
            P(None, "shard"),
            P(None, "shard"),
            P(None, "shard"),
        ),
        check_vma=False,
    )
```

profile of v0, /device:TPU:0, one launch (start us, length us, event | category | flops | bytes accessed | tf_op | source)
XLA Modules:
  0.0 246.3 jit_solution(11997030103826953133)
XLA Ops:
  7.2 0.0 reduce-scatter.5.cloned.1.call-start
  7.2 10.0 %convolution_multiply_fusion = f32[1280,1280]{1,0:T(8,128)} fusion(bf16[1536,1280]{1,0:T(8,128)(2,1)} %param.10, bf16[1536,1280]{1,0:T(8,128)(2,1)} %param.9), kind=kOutput, calls=%fused_computation | convolution fusion | flops 5034803200 | bytes 14417920 | tf_op jit(solution)/shard_map/dot_general | solution.py:49
  17.2 0.0 copy-start.6
  17.2 0.0 copy-start
  17.2 0.0 copy-start.1
  17.3 0.0 copy-start.2
  17.3 0.0 reduce-scatter.5.cloned.1.call-update
  17.3 0.0 reduce-scatter.7.cloned.1.call-start
  17.3 0.6 copy-done.4
  17.9 1.1 copy.19
  19.0 0.0 reduce-scatter.7.cloned.1.call-update
  19.0 0.0 all-reduce.3.cloned.1.call-start
  19.1 73.3 %reduce-scatter.5.cloned.1.call-done = f32[160,1280]{1,0:T(8,128)} async-done(((f32[1280,1280]{1,0:T(8,128)}), f32[160,1280]{1,0:T(8,128)}) %reduce-scatter.5.cloned.1.call-update) | async-done | bytes 819216 | tf_op jit(solution)/shard_map/reduce_scatter | solution.py:53
  92.4 0.0 all-reduce.3.cloned.1.call-update
  92.4 0.0 all-gather.3.cloned.1.call-start
  92.4 32.9 %reduce-scatter.7.cloned.1.call-done = f32[160,2]{1,0:T(8,128)} async-done(((f32[1280,2]{1,0:T(8,128)}), f32[160,2]{1,0:T(8,128)}) %reduce-scatter.7.cloned.1.call-update) | async-done | bytes 1296
  125.3 1.0 copy.20
  126.3 9.9 %psum.46 = f32[2,160]{1,0:T(2,128)S(1)} all-reduce(f32[2,160]{1,0:T(2,128)S(1)} %bitcast.15), channel_id=1, replica_groups=mesh['rep'=4,'shard'=8] {'rep'}, use_global_device_ids=true, to_apply=%region_10.0 | all-reduce | flops 320 | bytes 2560 | tf_op jit(solution)/shard_map/psum | solution.py:56
  136.2 0.0 copy-done.3
  136.2 0.7 multiply_reduce_fusion.3
  136.9 39.0 %all-reduce.3.cloned.1.call-done = f32[160,1280]{1,0:T(8,128)} async-done(((f32[160,1280]{1,0:T(8,128)}), f32[160,1280]{1,0:T(8,128)}) %all-reduce.3.cloned.1.call-update) | async-done | bytes 819216 | tf_op jit(solution)/shard_map/psum | solution.py:56
  175.9 0.0 copy-done.1
  175.9 3.6 %multiply_reduce_fusion.1 = (f32[]{:T(128)}, f32[160,1280]{1,0:T(8,128)S(1)}, f32[160,1280]{1,0:T(8,128)}, f32[160,1280]{1,0:T(8,128)}, f32[]{:T(128)}) fusion(f32[160,1280]{1,0:T(8,128)S(1)} %copy-done, f32[160,1280]{1,0:T(8,128)} %all-reduce.3.cloned.1.call-done, f32[160,1280]{1,0:T(8,128)S(1)} %copy-done.1, f32[160,1280]{1,0:T(8,128)S(1)} %copy-done.2), kind=kLoop, calls=%fused_computation.5 | loop fusion | flops 3481598 | bytes 5734408 | tf_op jit(solution)/shard_map/reduce_sum | solution.py:62
  179.5 16.8 %all-reduce = (f32[]{:T(128)}, f32[]{:T(128)}, f32[2]{0:T(128)S(1)}, f32[2]{0:T(128)S(1)}) all-reduce(f32[]{:T(128)} %get-tuple-element.24, f32[]{:T(128)} %get-tuple-element.20, f32[2]{0:T(128)S(1)} %get-tuple-element.16, f32[2]{0:T(128)S(1)} %get-tuple-element.25), channel_id=1, replica_groups=mesh['rep'=4,'shard'=8] {'shard'}, use_global_device_ids=true, to_apply=%region_1.0 | all-reduce | flops 6 | bytes 48 | tf_op jit(solution)/shard_map/psum | solution.py:45
  197.7 0.2 multiply_reduce_fusion
  197.9 1.2 fusion.2
  199.2 0.0 all-gather.3.cloned.1.call-update
  199.2 0.7 convert_bitcast_fusion
  199.9 8.4 %all-gather = bf16[8,160,2]{1,2,0:T(2,128)(2,1)S(1)} all-gather(bf16[1,160,2]{1,2,0:T(2,128)(2,1)S(1)} %get-tuple-element.12), channel_id=1, replica_groups=mesh['rep'=4,'shard'=8] {'shard'}, dimensions={0}, use_global_device_ids=true | all-gather | bytes 5760 | tf_op jit(solution)/shard_map/all_gather | solution.py:72
  208.3 0.7 reshape.30
  209.0 26.9 %all-gather.3.cloned.1.call-done = bf16[1280,1280]{1,0:T(8,128)(2,1)} async-done(((bf16[160,1280]{1,0:T(8,128)(2,1)}), bf16[1280,1280]{1,0:T(8,128)(2,1)}) %all-gather.3.cloned.1.call-update) | async-done | bytes 3276816 | tf_op jit(solution)/shard_map/all_gather | solution.py:71
  235.9 3.8 %copy.23 = bf16[1280,1280]{1,0:T(8,128)(2,1)} copy(bf16[1280,1280]{1,0:T(8,128)(2,1)} %all-gather.3.cloned.1.call-done) | data formatting | bytes 6553600
  (11 shorter events, 0.0 us)
Async XLA Ops:
  7.2 85.2 %reduce-scatter.5.cloned.1.call-start = ((), (), s32[]{:S(2)}) async-start(), calls=%async_computation.2 | async-start | bytes 7372800 | tf_op jit(solution)/shard_map/reduce_scatter | solution.py:53
  17.2 0.7 copy-start.4
  17.2 119.0 %copy-start.3 = (f32[2,160]{1,0:T(2,128)S(1)}, f32[2,160]{1,0:T(2,128)}, u32[]{:S(2)}) copy-start(f32[2,160]{1,0:T(2,128)} %param.15) | copy-start | bytes 3844
  17.2 119.0 %copy-start.5 = (f32[2,160]{1,0:T(2,128)S(1)}, f32[2,160]{1,0:T(2,128)}, u32[]{:S(2)}) copy-start(f32[2,160]{1,0:T(2,128)} %param.16) | copy-start | bytes 3844
  17.2 119.0 %copy-start.6 = (f32[2,160]{1,0:T(2,128)S(1)}, f32[2,160]{1,0:T(2,128)}, u32[]{:S(2)}) copy-start(f32[2,160]{1,0:T(2,128)} %param.17) | copy-start | bytes 3844
  17.2 158.7 %copy-start = (f32[160,1280]{1,0:T(8,128)S(1)}, f32[160,1280]{1,0:T(8,128)}, u32[]{:S(2)}) copy-start(f32[160,1280]{1,0:T(8,128)} %param.12) | copy-start | bytes 2457604
  17.2 158.7 %copy-start.1 = (f32[160,1280]{1,0:T(8,128)S(1)}, f32[160,1280]{1,0:T(8,128)}, u32[]{:S(2)}) copy-start(f32[160,1280]{1,0:T(8,128)} %param.13) | copy-start | bytes 2457604
  17.3 158.7 %copy-start.2 = (f32[160,1280]{1,0:T(8,128)S(1)}, f32[160,1280]{1,0:T(8,128)}, u32[]{:S(2)}) copy-start(f32[160,1280]{1,0:T(8,128)} %param.14) | copy-start | bytes 2457604
  17.3 108.0 %reduce-scatter.7.cloned.1.call-start = ((), (), s32[]{:S(2)}) async-start(), calls=%async_computation.5 | async-start | bytes 737280
  19.0 156.9 %all-reduce.3.cloned.1.call-start = ((), (), s32[]{:S(2)}) async-start(), calls=%async_computation.3 | async-start | bytes 1638400 | tf_op jit(solution)/shard_map/psum | solution.py:56
  92.4 143.5 %all-gather.3.cloned.1.call-start = ((), (), s32[]{:S(2)}) async-start(), calls=%async_computation.4 | async-start | bytes 3686400 | tf_op jit(solution)/shard_map/all_gather | solution.py:71
Sparse Core Ops, SparseCore 0:
  17.4 74.9 reduce-scatter.4
  95.2 30.0 reduce-scatter.6
  128.4 47.4 all-reduce.2
  199.3 36.5 all-gather.2
where the time goes:
time: 247 us; the launch traced here: 246 us
  waiting for transfers between devices  172 us (70%)
  blocking collectives  35.1 us (14%)
  between operations  15.2 us (6%)
  matrix products  10 us (4%)
  local copies, waits for them, and re-layouts  7.19 us (3%)
  other arithmetic  6.45 us (3%)
    reduce_scatter x1, waiting for transfers between devices, per_device(): lax.psum_scatter(grad_term, 'shard', scatter_dimension=0, tiled=True)  73.3 us
    psum x1, waiting for transfers between devices, per_device(): grad_rows, grad_columns = lax.psum((shard_grad, shard_vector), 'rep')  39 us
    unnamed x5, waiting for transfers between devices  33 us
    all_gather x1, waiting for transfers between devices, per_device(): lax.all_gather(master_rows.astype(jnp.bfloat16), 'shard', axis=0, tiled=T...  26.9 us
    psum x1, blocking collectives, per_device(): weight_tot, vector_tot = lax.psum((weight_sq, vector_sq), 'shard')  16.8 us
    dot_general x1, matrix products, per_device(): lax.dot_general(cotangents, activations, contract, preferred_element_type...  10 us
    psum x1, blocking collectives, per_device(): grad_rows, grad_columns = lax.psum((shard_grad, shard_vector), 'rep')  9.91 us
    all_gather x1, blocking collectives, per_device(): lax.all_gather(master_vecs.astype(jnp.bfloat16), 'shard', axis=1, tiled=T...  8.42 us
  transfers between devices with their start and end apart: 4, of which 4 were waited for; matrix products, arithmetic and copies ran while one was open for 2% of the time, Pallas kernels for 0%

commit v1 on v0

--- a/solution.py
+++ b/solution.py
@@ -39,38 +39,48 @@
     rep_count = lax.axis_size("rep")
     shard_count = lax.axis_size("shard")
     tok_count, model_width = activations.shape
+    rows = master_matrix.shape[0]
     grad_scale = 1.0 / math.sqrt(tok_count * rep_count * shard_count)
     weight_sq = jnp.sum(master_matrix * master_matrix)
     vector_sq = jnp.sum(master_vector * master_vector, axis=1)
-    weight_tot, vector_tot = lax.psum((weight_sq, vector_sq), "shard")
-    vector_term = grad_vectors[0].astype(jnp.float32).T * grad_scale
     contract = (((0,), (0,)), ((), ()))
     grad_term = (
         lax.dot_general(cotangents, activations, contract, preferred_element_type=jnp.float32)
         * grad_scale
     )
-    shard_grad, shard_vector = (
-        lax.psum_scatter(grad_term, "shard", scatter_dimension=0, tiled=True),
-        lax.psum_scatter(vector_term, "shard", scatter_dimension=0, tiled=True),
-    )
-    grad_rows, grad_columns = lax.psum((shard_grad, shard_vector), "rep")
-    grad_vecs = grad_columns.T
+    vector_term = grad_vectors[0].astype(jnp.float32) * grad_scale
+    vector_rows = vector_term.reshape(2, shard_count, rows).transpose(1, 0, 2)
+    vector_rows = vector_rows.reshape(shard_count, 1, 2 * rows)
+    vector_rows = jnp.pad(vector_rows, ((0, 0), (0, 7), (0, model_width - 2 * rows)))
+    blocks = jnp.concatenate(
+        [grad_term.reshape(shard_count, rows, model_width), vector_rows], axis=1
+    ).reshape(shard_count * (rows + 8), model_width)
+    shard_grad = lax.psum_scatter(blocks, "shard", scatter_dimension=0, tiled=True)
+    summed = lax.psum(shard_grad, "rep")
+    grad_rows = summed[:rows]
+    grad_vecs = summed[rows, : 2 * rows].reshape(2, rows)
     first_rows, second_rows = moments(grad_rows, first_matrix, second_matrix)
     first_vecs, second_vecs = moments(grad_vecs, first_vector, second_vector)
     update_matrix = direction_of(first_rows, second_rows, master_matrix)
     update_vec = direction_of(first_vecs, second_vecs, master_vector)
     update_sq = jnp.sum(update_matrix * update_matrix)
     upvector_sq = jnp.sum(update_vec * update_vec, axis=1)
-    update_tot, upvector_tot = lax.psum((update_sq, upvector_sq), "shard")
+    weight_tot, vector_tot, update_tot, upvector_tot = lax.psum(
+        (weight_sq, vector_sq, update_sq, upvector_sq), "shard"
+    )
     trust_matrix = jnp.sqrt(weight_tot) / jnp.sqrt(update_tot + norm_eps)
     trust_vec = (jnp.sqrt(vector_tot) / jnp.sqrt(upvector_tot + norm_eps))[:, None]
     stepped = master_matrix - learn_rate * trust_matrix * update_matrix
     master_rows = stepped / jnp.sqrt(jnp.mean(stepped * stepped, axis=1, keepdims=True) + norm_eps)
     master_vecs = master_vector - learn_rate * trust_vec * update_vec
-    gathered_matrix, gathered_vectors = (
-        lax.all_gather(master_rows.astype(jnp.bfloat16), "shard", axis=0, tiled=True),
-        lax.all_gather(master_vecs.astype(jnp.bfloat16), "shard", axis=1, tiled=True),
-    )
+    vec_row = master_vecs.astype(jnp.bfloat16).reshape(1, 2 * rows)
+    vec_row = jnp.pad(vec_row, ((0, 15), (0, model_width - 2 * rows)))
+    send = jnp.concatenate([master_rows.astype(jnp.bfloat16), vec_row], axis=0)
+    gathered = lax.all_gather(send, "shard", axis=0, tiled=True)
+    gathered = gathered.reshape(shard_count, rows + 16, model_width)
+    gathered_matrix = gathered[:, :rows].reshape(shard_count * rows, model_width)
+    gathered_vectors = gathered[:, rows, : 2 * rows].reshape(shard_count, 2, rows)
+    gathered_vectors = gathered_vectors.transpose(1, 0, 2).reshape(2, shard_count * rows)
     return (
         gathered_matrix,
         gathered_vectors,

time: 247 us -> 228 us (0.923)
  blocking collectives: 35.1 us -> 16.8 us
  other arithmetic: 6.45 us -> 11.1 us
  waiting for transfers between devices: 172 us -> 169 us
    unnamed x5 -> x3, waiting for transfers between devices: 33 us -> 0.05 us
    all_gather x1, waiting for transfers between devices: 26.9 us -> 39.6 us  [per_device(): gathered = lax.all_gather(send, 'shard', axis=0, tiled=True)]
    psum x1, waiting for transfers between devices: 39 us -> 51.4 us  [per_device(): summed = lax.psum(shard_grad, 'rep')]
    psum x2 -> x1, blocking collectives: 26.7 us -> 16.8 us  [per_device(): lax.psum((weight_sq, vector_sq, update_sq, upvector_sq), 'shard')]
    all_gather x1 -> x0, blocking collectives: 8.42 us -> none  [per_device(): lax.all_gather(master_vecs.astype(jnp.bfloat16), 'shard', axis=1, tiled=T...]
    unnamed x18 -> x13, local copies, waits for them, and re-layouts: 7.18 us -> 0.03 us
    slice x0 -> x3, local copies, waits for them, and re-layouts: none -> 5.38 us  [the longest x1 3.85 us: per_device(): gathered[:, :rows].reshape(shard_count * rows, model_width)]
    reduce_scatter x1, waiting for transfers between devices: 73.3 us -> 78.1 us  [per_device(): lax.psum_scatter(blocks, 'shard', scatter_dimension=0, tiled=True)]
  transfers between devices with their start and end apart: 4 -> 3, of which waited for: 4 -> 3; matrix products, arithmetic and copies ran while one was open for 2% -> 0% of each run, Pallas kernels for 0% -> 0%
where the time goes in v1:
time: 228 us
  waiting for transfers between devices  169 us (74%)
  blocking collectives  16.8 us (7%)
  between operations  15.2 us (7%)
  other arithmetic  11.1 us (5%)
  matrix products  8.86 us (4%)
  local copies, waits for them, and re-layouts  6.56 us (3%)
    reduce_scatter x1, waiting for transfers between devices, per_device(): lax.psum_scatter(blocks, 'shard', scatter_dimension=0, tiled=True)  78.1 us
    psum x1, waiting for transfers between devices, per_device(): summed = lax.psum(shard_grad, 'rep')  51.4 us
    all_gather x1, waiting for transfers between devices, per_device(): gathered = lax.all_gather(send, 'shard', axis=0, tiled=True)  39.6 us
    psum x1, blocking collectives, per_device(): lax.psum((weight_sq, vector_sq, update_sq, upvector_sq), 'shard')  16.8 us
    dot_general x1, matrix products, per_device(): lax.dot_general(cotangents, activations, contract, preferred_element_type...  8.86 us
  transfers between devices with their start and end apart: 3, of which 3 were waited for; matrix products, arithmetic and copies ran while one was open for 0% of the time, Pallas kernels for 0%

profile of v1, /device:TPU:0, one launch (start us, length us, event | category | flops | bytes accessed | tf_op | source)
XLA Modules:
  0.0 227.9 jit_solution(3295873730353829676)
XLA Ops:
  7.2 0.0 reduce-scatter.2.cloned.1.call-start
  7.2 0.7 convert_multiply_fusion
  7.9 0.1 mul.113
  8.0 0.1 reshape.53
  8.1 8.9 %convolution_multiply_fusion = f32[1280,1280]{1,0:T(8,128)S(1)} fusion(bf16[1536,1280]{1,0:T(8,128)(2,1)} %param.10, bf16[1536,1280]{1,0:T(8,128)(2,1)} %param.9), kind=kOutput, calls=%fused_computation | convolution fusion | flops 5034803200 | bytes 14417920 | tf_op jit(solution)/shard_map/dot_general | solution.py:48
  17.0 3.3 %select_maximum_fusion = f32[8,168,1280]{2,1,0:T(8,128)} fusion(f32[8,1,320]{2,1,0:T(1,128)S(1)} %reshape.53, f32[8,160,1280]{2,1,0:T(8,128)S(1)} %bitcast.11), kind=kLoop, calls=%fused_computation.1 | loop fusion | flops 5160960 | bytes 13445120 | tf_op jit(solution)/shard_map/concatenate | solution.py:55
  20.3 0.0 copy-start.1
  20.3 0.0 copy-start.2
  20.3 0.0 reduce-scatter.2.cloned.1.call-update
  20.3 0.0 all-reduce.5.cloned.1.call-start
  20.4 78.1 %reduce-scatter.2.cloned.1.call-done = f32[168,1280]{1,0:T(8,128)} async-done(((f32[1344,1280]{1,0:T(8,128)}), f32[168,1280]{1,0:T(8,128)}) %reduce-scatter.2.cloned.1.call-update) | async-done | bytes 860176 | tf_op jit(solution)/shard_map/reduce_scatter | solution.py:58
  98.5 0.0 all-reduce.5.cloned.1.call-update
  98.6 0.0 all-gather.2.cloned.1.call-start
  98.6 51.4 %all-reduce.5.cloned.1.call-done = f32[168,1280]{1,0:T(8,128)} async-done(((f32[168,1280]{1,0:T(8,128)}), f32[168,1280]{1,0:T(8,128)}) %all-reduce.5.cloned.1.call-update) | async-done | bytes 860176 | tf_op jit(solution)/shard_map/psum | solution.py:59
  150.0 0.7 slice_reduce_fusion
  150.8 0.1 reshape_squeeze.6
  150.9 0.0 copy-done.4
  150.9 0.7 multiply_reduce_fusion.3
  151.6 0.0 copy-done.1
  151.6 3.6 %multiply_reduce_fusion.1 = (f32[]{:T(128)}, f32[160,1280]{1,0:T(8,128)S(1)}, f32[160,1280]{1,0:T(8,128)}, f32[160,1280]{1,0:T(8,128)}, f32[]{:T(128)}) fusion(f32[160,1280]{1,0:T(8,128)S(1)} %copy-done, f32[168,1280]{1,0:T(8,128)} %all-reduce.5.cloned.1.call-done, f32[160,1280]{1,0:T(8,128)S(1)} %copy-done.1, f32[160,1280]{1,0:T(8,128)S(1)} %copy-done.2), kind=kLoop, calls=%fused_computation.9 | loop fusion | flops 3481598 | bytes 5734408 | tf_op jit(solution)/shard_map/reduce_sum | solution.py:66
  155.2 16.8 %all-reduce.2 = (f32[2]{0:T(128)S(1)}, f32[2]{0:T(128)S(1)}, f32[]{:T(128)}, f32[]{:T(128)}) all-reduce(f32[2]{0:T(128)S(1)} %get-tuple-element.20, f32[2]{0:T(128)S(1)} %get-tuple-element.25, f32[]{:T(128)} %get-tuple-element.24, f32[]{:T(128)} %get-tuple-element.16), channel_id=1, replica_groups=mesh['rep'=4,'shard'=8] {'shard'}, use_global_device_ids=true, to_apply=%region_10.11 | all-reduce | flops 6 | bytes 48 | tf_op jit(solution)/shard_map/psum | solution.py:68
  173.4 0.7 fusion.5
  174.1 0.1 reshape.55
  174.1 0.2 multiply_reduce_fusion
  174.4 1.1 fusion.4
  175.5 0.8 fusion.2
  176.3 0.0 all-gather.2.cloned.1.call-update
  176.3 39.6 %all-gather.2.cloned.1.call-done = bf16[1408,1280]{1,0:T(8,128)(2,1)} async-done(((bf16[176,1280]{1,0:T(8,128)(2,1)}), bf16[1408,1280]{1,0:T(8,128)(2,1)}) %all-gather.2.cloned.1.call-update) | async-done | bytes 3604496 | tf_op jit(solution)/shard_map/all_gather | solution.py:79
  215.9 0.8 slice.19
  216.7 3.8 %slice.18 = bf16[8,160,1280]{2,1,0:T(8,128)(2,1)} slice(bf16[8,176,1280]{2,1,0:T(8,128)(2,1)} %bitcast.14), slice={[0:8], [0:160], [0:1280]} | slice | bytes 6553600 | tf_op jit(solution)/shard_map/slice | solution.py:81
  220.6 0.1 reshape_squeeze.7
  220.7 0.7 reshape.58
  (13 shorter events, 0.1 us)
Async XLA Ops:
  7.2 91.4 %reduce-scatter.2.cloned.1.call-start = ((), (), s32[]{:S(2)}) async-start(), calls=%async_computation.1 | async-start | bytes 7741440 | tf_op jit(solution)/shard_map/reduce_scatter | solution.py:58
  20.3 130.6 %copy-start.3 = (f32[2,160]{1,0:T(2,128)S(1)}, f32[2,160]{1,0:T(2,128)}, u32[]{:S(2)}) copy-start(f32[2,160]{1,0:T(2,128)} %param.15) | copy-start | bytes 3844
  20.3 130.6 %copy-start.4 = (f32[2,160]{1,0:T(2,128)S(1)}, f32[2,160]{1,0:T(2,128)}, u32[]{:S(2)}) copy-start(f32[2,160]{1,0:T(2,128)} %param.16) | copy-start | bytes 3844
  20.3 130.6 %copy-start.5 = (f32[2,160]{1,0:T(2,128)S(1)}, f32[2,160]{1,0:T(2,128)}, u32[]{:S(2)}) copy-start(f32[2,160]{1,0:T(2,128)} %param.17) | copy-start | bytes 3844
  20.3 131.3 %copy-start = (f32[160,1280]{1,0:T(8,128)S(1)}, f32[160,1280]{1,0:T(8,128)}, u32[]{:S(2)}) copy-start(f32[160,1280]{1,0:T(8,128)} %param.12) | copy-start | bytes 2457604
  20.3 131.3 %copy-start.1 = (f32[160,1280]{1,0:T(8,128)S(1)}, f32[160,1280]{1,0:T(8,128)}, u32[]{:S(2)}) copy-start(f32[160,1280]{1,0:T(8,128)} %param.13) | copy-start | bytes 2457604
  20.3 131.3 %copy-start.2 = (f32[160,1280]{1,0:T(8,128)S(1)}, f32[160,1280]{1,0:T(8,128)}, u32[]{:S(2)}) copy-start(f32[160,1280]{1,0:T(8,128)} %param.14) | copy-start | bytes 2457604
  20.3 129.7 %all-reduce.5.cloned.1.call-start = ((), (), s32[]{:S(2)}) async-start(), calls=%async_computation.2 | async-start | bytes 1720320 | tf_op jit(solution)/shard_map/psum | solution.py:59
  98.6 117.4 %all-gather.2.cloned.1.call-start = ((), (), s32[]{:S(2)}) async-start(), calls=%async_computation.3 | async-start | bytes 4055040 | tf_op jit(solution)/shard_map/all_gather | solution.py:79
Sparse Core Ops, SparseCore 0:
  20.5 78.0 reduce-scatter.1
  101.7 48.3 all-reduce.4
  176.4 39.4 all-gather.1

commit v2 on v1

--- a/solution.py
+++ b/solution.py
@@ -25,6 +25,73 @@
     return fresh_one / bias_one / (jnp.sqrt(fresh_two / bias_two) + adam_eps) + decay_rate * master
 
 
+def _bit(value, k):
+    return (value >> k) & 1
+
+
+def _exchange(x, pairs):
+    return lax.ppermute(x, ("rep", "shard"), pairs)
+
+
+def _reduce_gradient(grad_term, rep_count, shard_count, rows):
+    total = rep_count * shard_count
+    chips = shard_count // 2
+    width = grad_term.shape[1]
+    rep_bits = rep_count.bit_length() - 1
+    chip_bits = chips.bit_length() - 1
+    slice_rows = rows // rep_count
+    rep_idx = lax.axis_index("rep")
+    shard_idx = lax.axis_index("shard")
+    core = shard_idx % 2
+    chip = shard_idx // 2
+
+    def core_of(i):
+        return (i % shard_count) % 2
+
+    split = grad_term.reshape(chips, 2, rows, width)
+    keep = lax.dynamic_index_in_dim(split, core, axis=1, keepdims=False)
+    send = lax.dynamic_index_in_dim(split, 1 - core, axis=1, keepdims=False)
+    held = keep + _exchange(send, [(i, i ^ 1) for i in range(total)])
+
+    orders = (list(range(rep_bits)), list(reversed(range(rep_bits))))
+    held = held.reshape(chips, rep_count, slice_rows, width)
+    picks = []
+    for j in range(rep_bits):
+        pick = jnp.where(core == 0, _bit(rep_idx, orders[0][j]), _bit(rep_idx, orders[1][j]))
+        picks.append(pick)
+        pairs = [(i, i ^ ((1 << orders[core_of(i)][j]) * shard_count)) for i in range(total)]
+        halves = held.reshape(chips, 2, -1, slice_rows, width)
+        keep = lax.dynamic_index_in_dim(halves, pick, axis=1, keepdims=False)
+        send = lax.dynamic_index_in_dim(halves, 1 - pick, axis=1, keepdims=False)
+        held = keep + _exchange(send, pairs)
+    held = held.reshape(chips, slice_rows, width)
+
+    for j in range(chip_bits):
+        pick = _bit(chip, j)
+        pairs = [(i, i ^ ((1 << j) * 2)) for i in range(total)]
+        halves = held.reshape(chips >> (j + 1), 2, slice_rows, width)
+        keep = lax.dynamic_index_in_dim(halves, pick, axis=1, keepdims=False)
+        send = lax.dynamic_index_in_dim(halves, 1 - pick, axis=1, keepdims=False)
+        held = keep + _exchange(send, pairs)
+    held = held.reshape(slice_rows, width)
+
+    for j in reversed(range(rep_bits)):
+        pick = picks[j]
+        pairs = [(i, i ^ ((1 << orders[core_of(i)][j]) * shard_count)) for i in range(total)]
+        other = _exchange(held, pairs)
+        low = jnp.where(pick == 0, held, other)
+        high = jnp.where(pick == 0, other, held)
+        held = jnp.concatenate([low[None], high[None]], axis=0).reshape(-1, width)
+    return held
+
+
+def _sum_over_shard(values, shard_count, rep_count):
+    total = rep_count * shard_count
+    for j in range(shard_count.bit_length() - 1):
+        values = values + _exchange(values, [(i, i ^ (1 << j)) for i in range(total)])
+    return values
+
+
 def per_device(
     activations,
     cotangents,
@@ -41,6 +108,9 @@
     tok_count, model_width = activations.shape
     rows = master_matrix.shape[0]
     grad_scale = 1.0 / math.sqrt(tok_count * rep_count * shard_count)
+    shard_idx = lax.axis_index("shard")
+    vector_term = grad_vectors[0].astype(jnp.float32) * grad_scale
+    vector_sum = lax.psum(vector_term, ("rep", "shard"))
     weight_sq = jnp.sum(master_matrix * master_matrix)
     vector_sq = jnp.sum(master_vector * master_vector, axis=1)
     contract = (((0,), (0,)), ((), ()))
@@ -48,26 +118,19 @@
         lax.dot_general(cotangents, activations, contract, preferred_element_type=jnp.float32)
         * grad_scale
     )
-    vector_term = grad_vectors[0].astype(jnp.float32) * grad_scale
-    vector_rows = vector_term.reshape(2, shard_count, rows).transpose(1, 0, 2)
-    vector_rows = vector_rows.reshape(shard_count, 1, 2 * rows)
-    vector_rows = jnp.pad(vector_rows, ((0, 0), (0, 7), (0, model_width - 2 * rows)))
-    blocks = jnp.concatenate(
-        [grad_term.reshape(shard_count, rows, model_width), vector_rows], axis=1
-    ).reshape(shard_count * (rows + 8), model_width)
-    shard_grad = lax.psum_scatter(blocks, "shard", scatter_dimension=0, tiled=True)
-    summed = lax.psum(shard_grad, "rep")
-    grad_rows = summed[:rows]
-    grad_vecs = summed[rows, : 2 * rows].reshape(2, rows)
+    grad_rows = _reduce_gradient(grad_term, rep_count, shard_count, rows)
+    grad_vecs = lax.dynamic_slice_in_dim(vector_sum, shard_idx * rows, rows, axis=1)
     first_rows, second_rows = moments(grad_rows, first_matrix, second_matrix)
     first_vecs, second_vecs = moments(grad_vecs, first_vector, second_vector)
     update_matrix = direction_of(first_rows, second_rows, master_matrix)
     update_vec = direction_of(first_vecs, second_vecs, master_vector)
     update_sq = jnp.sum(update_matrix * update_matrix)
     upvector_sq = jnp.sum(update_vec * update_vec, axis=1)
-    weight_tot, vector_tot, update_tot, upvector_tot = lax.psum(
-        (weight_sq, vector_sq, update_sq, upvector_sq), "shard"
+    sums = jnp.concatenate(
+        [weight_sq[None], vector_sq, update_sq[None], upvector_sq]
     )
+    sums = _sum_over_shard(sums, shard_count, rep_count)
+    weight_tot, vector_tot, update_tot, upvector_tot = sums[0], sums[1:3], sums[3], sums[4:6]
     trust_matrix = jnp.sqrt(weight_tot) / jnp.sqrt(update_tot + norm_eps)
     trust_vec = (jnp.sqrt(vector_tot) / jnp.sqrt(upvector_tot + norm_eps))[:, None]
     stepped = master_matrix - learn_rate * trust_matrix * update_matrix

time: 228 us -> 210 us (0.921)
  waiting for transfers between devices: 169 us -> 105 us
  blocking collectives: 16.8 us -> 40.9 us
  starting transfers between devices: 0.12 us -> 14.6 us
  local copies, waits for them, and re-layouts: 6.56 us -> 11.4 us
  other arithmetic: 11.1 us -> 14 us
    reduce_scatter x1 -> x0, waiting for transfers between devices: 78.1 us -> none  [per_device(): lax.psum_scatter(blocks, 'shard', scatter_dimension=0, tiled=True)]
    ppermute x0 -> x10, waiting for transfers between devices: none -> 63.1 us  [_exchange(): return lax.ppermute(x, ('rep', 'shard'), pairs)]
    psum x1 -> x0, waiting for transfers between devices: 51.4 us -> none  [per_device(): summed = lax.psum(shard_grad, 'rep')]
    psum x1, blocking collectives: 16.8 us -> 40.9 us  [per_device(): vector_sum = lax.psum(vector_term, ('rep', 'shard'))]
    ppermute x0 -> x10, starting transfers between devices: none -> 14.6 us  [_exchange(): return lax.ppermute(x, ('rep', 'shard'), pairs)]
    add x0 -> x7, other arithmetic: none -> 6.23 us  [the longest x1 3.31 us: _reduce_gradient(): held = keep + _exchange(send, [(i, i ^ 1) for i in range(total)])]
    unnamed x13 -> x19, local copies, waits for them, and re-layouts: 0.03 us -> 3.58 us
  transfers between devices with their start and end apart: 3 -> 11, of which waited for: 3 -> 10; matrix products, arithmetic and copies ran while one was open for 0% -> 0% of each run, Pallas kernels for 0% -> 0%
where the time goes in v2:
time: 210 us
  waiting for transfers between devices  105 us (50%)
  blocking collectives  40.9 us (19%)
  between operations  15.6 us (7%)
  starting transfers between devices  14.6 us (7%)
  other arithmetic  14 us (7%)
  local copies, waits for them, and re-layouts  11.4 us (5%)
  matrix products  8.65 us (4%)
    ppermute x10, waiting for transfers between devices, _exchange(): return lax.ppermute(x, ('rep', 'shard'), pairs)  63.1 us
    all_gather x1, waiting for transfers between devices, per_device(): gathered = lax.all_gather(send, 'shard', axis=0, tiled=True)  41.6 us
    psum x1, blocking collectives, per_device(): vector_sum = lax.psum(vector_term, ('rep', 'shard'))  40.9 us
    ppermute x10, starting transfers between devices, _exchange(): return lax.ppermute(x, ('rep', 'shard'), pairs)  14.6 us
    dot_general x1, matrix products, per_device(): lax.dot_general(cotangents, activations, contract, preferred_element_type...  8.65 us
  transfers between devices with their start and end apart: 11, of which 10 were waited for; matrix products, arithmetic and copies ran while one was open for 0% of the time, Pallas kernels for 0%

profile of v2, /device:TPU:0, one launch (start us, length us, event | category | flops | bytes accessed | tf_op | source)
XLA Modules:
  0.0 209.8 jit_solution(15398459512062660843)
XLA Ops:
  7.2 8.6 %convolution_multiply_fusion = f32[1280,1280]{1,0:T(8,128)S(1)} fusion(bf16[1536,1280]{1,0:T(8,128)(2,1)} %param.10, bf16[1536,1280]{1,0:T(8,128)(2,1)} %param.9), kind=kOutput, calls=%fused_computation | convolution fusion | flops 5034803200 | bytes 14417920 | tf_op jit(solution)/shard_map/dot_general | solution.py:118
  16.2 2.4 %copy-done.1 = f32[1280,1280]{1,0:T(8,128)} copy-done((f32[1280,1280]{1,0:T(8,128)}, f32[1280,1280]{1,0:T(8,128)S(1)}, u32[]{:S(2)}) %copy-start.1) | copy-done | bytes 6553624
  19.1 5.6 %collective-permute-done = f32[4,160,1280]{2,1,0:T(8,128)} collective-permute-done((f32[4,160,1280]{2,1,0:T(8,128)S(1)}, f32[4,160,1280]{2,1,0:T(8,128)}, u32[]{:S(2)}, u32[]{:S(2)}) %collective-permute-start) | collective-permute-done | bytes 3276832 | tf_op jit(solution)/shard_map/ppermute | solution.py:33
  24.7 3.3 %bitcast_add_fusion = f32[4,160,1280]{2,1,0:T(8,128)S(1)} fusion(f32[4,160,1280]{2,1,0:T(8,128)} %collective-permute-done, f32[4,2,160,1280]{3,2,1,0:T(8,128)} %bitcast.50, s32[]{:T(128)S(6)} %select_n.84), kind=kLoop, calls=%fused_computation.1 | loop fusion | flops 819200 | bytes 9830404 | tf_op jit(solution)/shard_map/add | solution.py:54
  28.0 1.3 dynamic-slice_bitcast_fusion.1
  29.3 2.8 %collective-permute-start.1 = (f32[4,2,40,1280]{3,2,1,0:T(8,128)}, f32[4,2,40,1280]{3,2,1,0:T(8,128)}, u32[]{:S(2)}, u32[]{:S(2)}) collective-permute-start(f32[4,2,40,1280]{3,2,1,0:T(8,128)} %dynamic-slice_bitcast_fusion.1), channel_id=1, source_target_pairs={{0,8},{1,17},{2,10},{3,19},{4,12},{5,21},{6,14},{7,23},{8,0},{9,25... | collective-permute-start | bytes 4915208 | tf_op jit(solution)/shard_map/ppermute | solution.py:33
  32.2 19.4 %collective-permute-done.1 = f32[4,2,40,1280]{3,2,1,0:T(8,128)} collective-permute-done((f32[4,2,40,1280]{3,2,1,0:T(8,128)}, f32[4,2,40,1280]{3,2,1,0:T(8,128)}, u32[]{:S(2)}, u32[]{:S(2)}) %collective-permute-start.1) | collective-permute-done | bytes 1638432 | tf_op jit(solution)/shard_map/ppermute | solution.py:33
  51.6 1.6 bitcast_add_fusion.1
  53.2 1.2 copy-done.2
  54.4 2.1 %collective-permute-start.2 = (f32[4,1,40,1280]{3,2,1,0:T(8,128)S(1)}, f32[4,1,40,1280]{3,2,1,0:T(8,128)S(1)}, u32[]{:S(2)}, u32[]{:S(2)}) collective-permute-start(f32[4,1,40,1280]{3,2,1,0:T(8,128)S(1)} %constant_dynamic-slice_fusion.2), channel_id=1, source_target_pairs={{0,16},{1,9},{2,18},{3,11},{4,20},{5,13},{6,22},{7,15},{8,24},{9,1... | collective-permute-start | bytes 2457608 | tf_op jit(solution)/shard_map/ppermute | solution.py:33
  56.6 10.3 %collective-permute-done.2 = f32[4,1,40,1280]{3,2,1,0:T(8,128)S(1)} collective-permute-done((f32[4,1,40,1280]{3,2,1,0:T(8,128)S(1)}, f32[4,1,40,1280]{3,2,1,0:T(8,128)S(1)}, u32[]{:S(2)}, u32[]{:S(2)}) %collective-permute-start.2) | collective-permute-done | bytes 819232 | tf_op jit(solution)/shard_map/ppermute | solution.py:33
  66.9 1.3 dynamic-slice_add_fusion
  68.2 2.1 %collective-permute-start.3 = (f32[2,40,1280]{2,1,0:T(8,128)S(1)}, f32[2,40,1280]{2,1,0:T(8,128)S(1)}, u32[]{:S(2)}, u32[]{:S(2)}) collective-permute-start(f32[2,40,1280]{2,1,0:T(8,128)S(1)} %dynamic-slice_bitcast_fusion.2), channel_id=1, source_target_pairs={{0,2},{1,3},{2,0},{3,1},{4,6},{5,7},{6,4},{7,5},{8,10},{9,11},{10,... | collective-permute-start | bytes 1228808 | tf_op jit(solution)/shard_map/ppermute | solution.py:33
  70.3 8.1 %collective-permute-done.3 = f32[2,40,1280]{2,1,0:T(8,128)S(1)} collective-permute-done((f32[2,40,1280]{2,1,0:T(8,128)S(1)}, f32[2,40,1280]{2,1,0:T(8,128)S(1)}, u32[]{:S(2)}, u32[]{:S(2)}) %collective-permute-start.3) | collective-permute-done | bytes 409632 | tf_op jit(solution)/shard_map/ppermute | solution.py:33
  78.5 2.8 %collective-permute-start.4 = (f32[1,40,1280]{2,1,0:T(8,128)S(1)}, f32[1,40,1280]{2,1,0:T(8,128)S(1)}, u32[]{:S(2)}, u32[]{:S(2)}) collective-permute-start(f32[1,40,1280]{2,1,0:T(8,128)S(1)} %constant_dynamic-slice_fusion.1), channel_id=1, source_target_pairs={{0,4},{1,5},{2,6},{3,7},{4,0},{5,1},{6,2},{7,3},{8,12},{9,13},{10,... | collective-permute-start | bytes 614408 | tf_op jit(solution)/shard_map/ppermute | solution.py:33
  81.3 7.4 %collective-permute-done.4 = f32[1,40,1280]{2,1,0:T(8,128)S(1)} collective-permute-done((f32[1,40,1280]{2,1,0:T(8,128)S(1)}, f32[1,40,1280]{2,1,0:T(8,128)S(1)}, u32[]{:S(2)}, u32[]{:S(2)}) %collective-permute-start.4) | collective-permute-done | bytes 204832 | tf_op jit(solution)/shard_map/ppermute | solution.py:33
  88.7 1.5 collective-permute-start.5
  90.2 4.4 %collective-permute-done.5 = f32[40,1280]{1,0:T(8,128)S(1)} collective-permute-done((f32[40,1280]{1,0:T(8,128)S(1)}, f32[40,1280]{1,0:T(8,128)S(1)}, u32[]{:S(2)}, u32[]{:S(2)}) %collective-permute-start.5) | collective-permute-done | bytes 204832 | tf_op jit(solution)/shard_map/ppermute | solution.py:33
  94.6 1.4 collective-permute-start.6
  96.1 40.9 %psum.7 = f32[2,1280]{1,0:T(2,128)S(1)} all-reduce(f32[2,1280]{1,0:T(2,128)S(1)} %multiply_bitcast_fusion), channel_id=1, replica_groups=mesh['rep'=4,'shard'=8] {'rep','shard'}, use_global_device_ids=true, to_apply=%region_3.4 | all-reduce | flops 2560 | bytes 20480 | tf_op jit(solution)/shard_map/psum | solution.py:113
  137.0 0.8 multiply_reduce_fusion.3
  137.9 2.4 %multiply_reduce_fusion.1 = (f32[]{:T(128)}, f32[160,1280]{1,0:T(8,128)S(1)}, f32[160,1280]{1,0:T(8,128)}, f32[160,1280]{1,0:T(8,128)}, f32[]{:T(128)}) fusion(f32[160,1280]{1,0:T(8,128)S(1)} %copy-done, f32[2,80,1280]{2,1,0:T(8,128)S(1)} %pad_maximum_fusion, f32[160,1280]{1,0:T(8,128)S(1)} %copy-done.3, f32[160,1280]{1,0:T(8,128)S(1)} %copy-done.4), kind=kLoop, calls=%fused_computation.14 | loop fusion | flops 3481598 | bytes 5734408 | tf_op jit(solution)/shard_map/reduce_sum | solution.py:127
  140.4 1.4 pad_maximum_fusion.2
  141.8 1.1 collective-permute-done.7
  143.1 3.4 %collective-permute-done.8 = f32[6]{0:T(128)S(1)} collective-permute-done((f32[6]{0:T(128)S(1)}, f32[6]{0:T(128)S(1)}, u32[]{:S(2)}, u32[]{:S(2)}) %collective-permute-start.8) | collective-permute-done | bytes 56 | tf_op jit(solution)/shard_map/ppermute | solution.py:33
  146.5 1.0 collective-permute-start.9
  147.5 3.4 %collective-permute-done.9 = f32[6]{0:T(128)S(1)} collective-permute-done((f32[6]{0:T(128)S(1)}, f32[6]{0:T(128)S(1)}, u32[]{:S(2)}, u32[]{:S(2)}) %collective-permute-start.9) | collective-permute-done | bytes 56 | tf_op jit(solution)/shard_map/ppermute | solution.py:33
  153.2 1.1 fusion.5
  155.1 0.8 fusion.3
  155.9 41.6 %all-gather.2.cloned.1.call-done = bf16[1408,1280]{1,0:T(8,128)(2,1)} async-done(((bf16[176,1280]{1,0:T(8,128)(2,1)}), bf16[1408,1280]{1,0:T(8,128)(2,1)}) %all-gather.2.cloned.1.call-update) | async-done | bytes 3604496 | tf_op jit(solution)/shard_map/all_gather | solution.py:142
  197.6 3.8 %slice.24 = bf16[8,160,1280]{2,1,0:T(8,128)(2,1)} slice(bf16[8,176,1280]{2,1,0:T(8,128)(2,1)} %bitcast.54), slice={[0:8], [0:160], [0:1280]} | slice | bytes 6553600 | tf_op jit(solution)/shard_map/slice | solution.py:144
  201.4 0.8 slice.25
  (46 shorter events, 3.9 us)
Async XLA Ops:
  7.2 190.4 %all-gather.2.cloned.1.call-start = ((), (), s32[]{:S(2)}) async-start(), calls=%async_computation | async-start | bytes 4055040 | tf_op jit(solution)/shard_map/all_gather | solution.py:142
  15.9 2.7 %copy-start.1 = (f32[1280,1280]{1,0:T(8,128)}, f32[1280,1280]{1,0:T(8,128)S(1)}, u32[]{:S(2)}) copy-start(f32[1280,1280]{1,0:T(8,128)S(1)} %convolution_multiply_fusion) | copy-start | bytes 19660804
  18.6 6.1 %collective-permute-start = (f32[4,160,1280]{2,1,0:T(8,128)S(1)}, f32[4,160,1280]{2,1,0:T(8,128)}, u32[]{:S(2)}, u32[]{:S(2)}) collective-permute-start(f32[4,160,1280]{2,1,0:T(8,128)S(1)} %dynamic-slice_bitcast_fusion), channel_id=1, source_target_pairs={{0,1},{1,0},{2,3},{3,2},{4,5},{5,4},{6,7},{7,6},{8,9},{9,8},{10,11... | collective-permute-start | bytes 9830408 | tf_op jit(solution)/shard_map/ppermute | solution.py:33
  29.3 22.3 %collective-permute-start.1 = (f32[4,2,40,1280]{3,2,1,0:T(8,128)}, f32[4,2,40,1280]{3,2,1,0:T(8,128)}, u32[]{:S(2)}, u32[]{:S(2)}) collective-permute-start(f32[4,2,40,1280]{3,2,1,0:T(8,128)} %dynamic-slice_bitcast_fusion.1), channel_id=1, source_target_pairs={{0,8},{1,17},{2,10},{3,19},{4,12},{5,21},{6,14},{7,23},{8,0},{9,25... | collective-permute-start | bytes 4915208 | tf_op jit(solution)/shard_map/ppermute | solution.py:33
  53.2 1.2 copy-start.2
  54.4 12.4 %collective-permute-start.2 = (f32[4,1,40,1280]{3,2,1,0:T(8,128)S(1)}, f32[4,1,40,1280]{3,2,1,0:T(8,128)S(1)}, u32[]{:S(2)}, u32[]{:S(2)}) collective-permute-start(f32[4,1,40,1280]{3,2,1,0:T(8,128)S(1)} %constant_dynamic-slice_fusion.2), channel_id=1, source_target_pairs={{0,16},{1,9},{2,18},{3,11},{4,20},{5,13},{6,22},{7,15},{8,24},{9,1... | collective-permute-start | bytes 2457608 | tf_op jit(solution)/shard_map/ppermute | solution.py:33
  56.6 39.5 %copy-start.6 = (bf16[1,2,1280]{2,1,0:T(2,128)(2,1)S(1)}, bf16[1,2,1280]{2,1,0:T(2,128)(2,1)}, u32[]{:S(2)}) copy-start(bf16[1,2,1280]{2,1,0:T(2,128)(2,1)} %param.11) | copy-start | bytes 15364
  56.6 80.4 %copy-start.5 = (f32[2,160]{1,0:T(2,128)S(1)}, f32[2,160]{1,0:T(2,128)}, u32[]{:S(2)}) copy-start(f32[2,160]{1,0:T(2,128)} %param.15) | copy-start | bytes 3844
  56.6 80.4 %copy-start.7 = (f32[2,160]{1,0:T(2,128)S(1)}, f32[2,160]{1,0:T(2,128)}, u32[]{:S(2)}) copy-start(f32[2,160]{1,0:T(2,128)} %param.16) | copy-start | bytes 3844
  56.6 80.4 %copy-start.8 = (f32[2,160]{1,0:T(2,128)S(1)}, f32[2,160]{1,0:T(2,128)}, u32[]{:S(2)}) copy-start(f32[2,160]{1,0:T(2,128)} %param.17) | copy-start | bytes 3844
  68.2 10.2 %collective-permute-start.3 = (f32[2,40,1280]{2,1,0:T(8,128)S(1)}, f32[2,40,1280]{2,1,0:T(8,128)S(1)}, u32[]{:S(2)}, u32[]{:S(2)}) collective-permute-start(f32[2,40,1280]{2,1,0:T(8,128)S(1)} %dynamic-slice_bitcast_fusion.2), channel_id=1, source_target_pairs={{0,2},{1,3},{2,0},{3,1},{4,6},{5,7},{6,4},{7,5},{8,10},{9,11},{10,... | collective-permute-start | bytes 1228808 | tf_op jit(solution)/shard_map/ppermute | solution.py:33
  78.4 59.5 %copy-start = (f32[160,1280]{1,0:T(8,128)S(1)}, f32[160,1280]{1,0:T(8,128)}, u32[]{:S(2)}) copy-start(f32[160,1280]{1,0:T(8,128)} %param.12) | copy-start | bytes 2457604
  78.4 59.5 %copy-start.3 = (f32[160,1280]{1,0:T(8,128)S(1)}, f32[160,1280]{1,0:T(8,128)}, u32[]{:S(2)}) copy-start(f32[160,1280]{1,0:T(8,128)} %param.13) | copy-start | bytes 2457604
  78.5 59.5 %copy-start.4 = (f32[160,1280]{1,0:T(8,128)S(1)}, f32[160,1280]{1,0:T(8,128)}, u32[]{:S(2)}) copy-start(f32[160,1280]{1,0:T(8,128)} %param.14) | copy-start | bytes 2457604
  78.5 10.2 %collective-permute-start.4 = (f32[1,40,1280]{2,1,0:T(8,128)S(1)}, f32[1,40,1280]{2,1,0:T(8,128)S(1)}, u32[]{:S(2)}, u32[]{:S(2)}) collective-permute-start(f32[1,40,1280]{2,1,0:T(8,128)S(1)} %constant_dynamic-slice_fusion.1), channel_id=1, source_target_pairs={{0,4},{1,5},{2,6},{3,7},{4,0},{5,1},{6,2},{7,3},{8,12},{9,13},{10,... | collective-permute-start | bytes 614408 | tf_op jit(solution)/shard_map/ppermute | solution.py:33
  88.7 5.8 %collective-permute-start.5 = (f32[40,1280]{1,0:T(8,128)S(1)}, f32[40,1280]{1,0:T(8,128)S(1)}, u32[]{:S(2)}, u32[]{:S(2)}) collective-permute-start(f32[40,1280]{1,0:T(8,128)S(1)} %add_bitcast_fusion), channel_id=1, source_target_pairs={{0,16},{1,9},{2,18},{3,11},{4,20},{5,13},{6,22},{7,15},{8,24},{9,1... | collective-permute-start | bytes 614408 | tf_op jit(solution)/shard_map/ppermute | solution.py:33
  94.6 43.2 %collective-permute-start.6 = (f32[80,1280]{1,0:T(8,128)S(1)}, f32[80,1280]{1,0:T(8,128)S(1)}, u32[]{:S(2)}, u32[]{:S(2)}) collective-permute-start(f32[80,1280]{1,0:T(8,128)S(1)} %bitcast.56), channel_id=1, source_target_pairs={{0,8},{1,17},{2,10},{3,19},{4,12},{5,21},{6,14},{7,23},{8,0},{9,25... | collective-permute-start | bytes 1228808 | tf_op jit(solution)/shard_map/ppermute | solution.py:33
  141.7 1.2 collective-permute-start.7
  142.9 3.6 %collective-permute-start.8 = (f32[6]{0:T(128)S(1)}, f32[6]{0:T(128)S(1)}, u32[]{:S(2)}, u32[]{:S(2)}) collective-permute-start(f32[6]{0:T(128)S(1)} %add.151), channel_id=1, source_target_pairs={{0,2},{1,3},{2,0},{3,1},{4,6},{5,7},{6,4},{7,5},{8,10},{9,11},{10,... | collective-permute-start | bytes 80 | tf_op jit(solution)/shard_map/ppermute | solution.py:33
  146.5 4.5 %collective-permute-start.9 = (f32[6]{0:T(128)S(1)}, f32[6]{0:T(128)S(1)}, u32[]{:S(2)}, u32[]{:S(2)}) collective-permute-start(f32[6]{0:T(128)S(1)} %add.152), channel_id=1, source_target_pairs={{0,4},{1,5},{2,6},{3,7},{4,0},{5,1},{6,2},{7,3},{8,12},{9,13},{10,... | collective-permute-start | bytes 80 | tf_op jit(solution)/shard_map/ppermute | solution.py:33
Sparse Core Ops, SparseCore 0:
  156.1 41.4 all-gather.1
